TPU v7x, 32 devices: a whole 2x2x4 slice. The times are simulated.
32 devices in a mesh: groups: 2 (over x), date: 8 (over z, y), row: 2 (over core).
Axes of the slice: x: 2, y: 2, z: 4, core: 2. Of those that a mesh axis runs over, the one named last changes fastest.
Arguments:
- scenes: bfloat16 [16, 4, 512, 1024], P(('groups', 'date'), None, 'row'), parts along dimension 0, may hold values from -6 to 6
- resample_taps: float32 [2, 4, 7], replicated, may hold values from 0 to 0.35
- clear_mask: int32 [16, 128, 8], P('groups', ('row', 'date')), parts along dimension 0, may hold values 0 or 1
Outputs:
- smooth_fine: bfloat16 [16, 4, 512, 1024], P('groups', None, ('row', 'date')), parts along dimension 0
- smooth_half: bfloat16 [16, 4, 256, 512], P('groups', None, ('row', 'date')), parts along dimension 0
- smooth_quarter: bfloat16 [16, 4, 128, 256], P('groups', None, ('row', 'date')), parts along dimension 0
There are 2 independent parts, one for each index of `groups`. A program takes and returns all parts, laid end to end along the dimension named above; an argument that names none is the same for every part. Nothing has to cross between parts.
Inputs may be any that keep to these rules, and one draw needn't show every extreme that they name: `clear_mask`: 1 marks a clear block, 0 a cloudy one.
All inputs are finite; a program needn't handle non-finite values.
Results may differ from a plain program's by a relative error of at most 0.005.
Values may be sent and summed in bfloat16 or wider, within the bound.
No kernel may reach another device: no remote copies, remote signals or barrier semaphores. Data moves between devices by JAX's collectives and lax.ppermute only.
A program may use at most 128 MiB of HBM per device.

v0:
```python
import math
import jax
import jax.numpy as jnp
from jax import lax
from jax.sharding import PartitionSpec as P

gap_weights = [math.exp(-((k - 4) ** 2) / 8.0) for k in range(9)]
savgol_coeffs = [c / 231.0 for c in [-21.0, 14.0, 39.0, 54.0, 59.0, 54.0, 39.0, 14.0, -21.0]]
pyramid_filter = [0.125, 0.375, 0.375, 0.125]


def padded(block, sides, width):
    for axis, dim in sides:
        count = lax.axis_size(axis)
        forward = [(i, i + 1) for i in range(count - 1)]
        backward = [(target, source) for source, target in forward]
        low = lax.ppermute(
            lax.slice_in_dim(block, block.shape[dim] - width, None, axis=dim), axis, forward
        )
        high = lax.ppermute(lax.slice_in_dim(block, 0, width, axis=dim), axis, backward)
        block = jnp.concatenate([low, block, high], axis=dim)
    return block


def valid_taps(values, taps, axis):
    count = values.shape[axis] - 6
    total = jnp.zeros(values.shape[:axis] + (count,) + values.shape[axis + 1 :], jnp.float32)
    for k in range(7):
        shape = [1] * values.ndim
        shape[-3] = taps.shape[0]
        total = total + taps[:, k].reshape(shape) * lax.slice_in_dim(values, k, k + count, 1, axis)
    return total


def column_resample(values, taps):
    width = values.shape[3]
    source = lax.broadcasted_iota(jnp.int32, (width, width), 0)
    target = lax.broadcasted_iota(jnp.int32, (width, width), 1)
    offset = source - target + 3
    table = jnp.zeros((taps.shape[0], width, width), jnp.float32)
    for k in range(7):
        table = table + taps[:, k][:, None, None] * (offset == k).astype(jnp.float32)[None]
    return jnp.einsum(
        "tbrc,bcd->tbrd", values.astype(jnp.float32), table, precision=lax.Precision.HIGHEST
    )


def halve_columns(values):
    width = values.shape[3]
    source = lax.broadcasted_iota(jnp.int32, (width, width // 2), 0)
    target = lax.broadcasted_iota(jnp.int32, (width, width // 2), 1)
    place = source - 2 * target + 1
    table = jnp.zeros((width, width // 2), jnp.float32)
    for p in range(4):
        table = table + pyramid_filter[p] * (place == p).astype(jnp.float32)
    return jnp.dot(values, table, precision=lax.Precision.HIGHEST)


def halve_rows(extended):
    pairs_count = extended.shape[2] // 2
    pairs = extended.reshape(extended.shape[:2] + (pairs_count, 2) + extended.shape[3:])
    even = pairs[:, :, :, 0]
    odd = pairs[:, :, :, 1]
    return (
        pyramid_filter[0] * even[:, :, :-1]
        + pyramid_filter[1] * odd[:, :, :-1]
        + pyramid_filter[2] * even[:, :, 1:]
        + pyramid_filter[3] * odd[:, :, 1:]
    )


def decimate_rim(extended):
    return halve_columns(halve_rows(extended))


def keep_rows(values, first, total):
    places = first + lax.iota(jnp.int32, values.shape[2])
    inside = (places >= 0) & (places < total)
    return jnp.where(inside[None, None, :, None], values, 0.0)


def smooth(level, clear):
    values = level.astype(jnp.float32)
    dates = values.shape[0]
    clear4 = clear[:, None]
    weight = 0.1 + 0.9 * clear4
    weighted = jnp.pad(weight * values, ((4, 4), (0, 0), (0, 0), (0, 0)))
    weight_pad = jnp.pad(weight, ((4, 4), (0, 0), (0, 0), (0, 0)))
    numer = jnp.zeros_like(values)
    denom = jnp.zeros_like(weight)
    for k in range(9):
        numer = numer + gap_weights[k] * weighted[k : k + dates]
        denom = denom + gap_weights[k] * weight_pad[k : k + dates]
    filled = clear4 * values + (1.0 - clear4) * (numer / denom)
    edged = jnp.pad(filled, ((4, 4), (0, 0), (0, 0), (0, 0)), mode="edge")
    result = jnp.zeros_like(values)
    for k in range(9):
        result = result + savgol_coeffs[k] * edged[k : k + dates]
    return result.astype(jnp.bfloat16)


def expand_mask(clear_mask, row_rep, col_rep):
    grown = jnp.repeat(jnp.repeat(clear_mask, row_rep, axis=1), col_rep, axis=2)
    return grown.astype(jnp.float32)


def local(scenes, resample_taps, clear_mask):
    rows = scenes.shape[2]
    extended = padded(scenes, (("row", 2),), 6)
    across = column_resample(extended, resample_taps[0])
    resampled_wide = valid_taps(across, resample_taps[1], 2)
    band_index = lax.axis_index("row")
    total_rows = rows * lax.axis_size("row")
    resampled_wide = keep_rows(resampled_wide, band_index * rows - 3, total_rows)
    half_wide = decimate_rim(resampled_wide)
    half_wide = keep_rows(half_wide, band_index * (rows // 2) - 1, total_rows // 2)
    resampled = resampled_wide[:, :, 3 : 3 + rows]
    half = half_wide[:, :, 1 : 1 + rows // 2]
    quarter = decimate_rim(half_wide)
    level_zero = resampled.astype(jnp.bfloat16)
    level_one = half.astype(jnp.bfloat16)
    level_two = quarter.astype(jnp.bfloat16)
    clear_fine = expand_mask(clear_mask, 4, 128)
    clear_half = expand_mask(clear_mask, 2, 64)
    clear_quarter = expand_mask(clear_mask, 1, 32)
    smooth_fine = smooth(
        lax.all_to_all(level_zero, "date", split_axis=2, concat_axis=0, tiled=True), clear_fine
    )
    smooth_half = smooth(
        lax.all_to_all(level_one, "date", split_axis=2, concat_axis=0, tiled=True), clear_half
    )
    smooth_quarter = smooth(
        lax.all_to_all(level_two, "date", split_axis=2, concat_axis=0, tiled=True), clear_quarter
    )
    return (smooth_fine, smooth_half, smooth_quarter)


def solution(mesh):
    in_specs = (P(("groups", "date"), None, "row", None), P(), P("groups", ("row", "date"), None))
    out_specs = (
        P("groups", None, ("row", "date"), None),
        P("groups", None, ("row", "date"), None),
        P("groups", None, ("row", "date"), None),
    )
    return jax.shard_map(local, mesh=mesh, in_specs=in_specs, out_specs=out_specs, check_vma=False)
```

profile of v0, /device:TPU:0, one launch (start us, length us, event | category | flops | bytes accessed | tf_op | source)
XLA Modules:
  0.0 176.9 jit_solution(12469758215546184341)
XLA Ops:
  1.5 2.4 %collective-permute-start = (bf16[1,4,6,1024]{3,2,1,0:T(8,128)(2,1)S(1)}, bf16[1,4,6,1024]{3,2,1,0:T(8,128)(2,1)S(1)}, u32[]{:S(2)}, u32[]{:S(2)}) collective-permute-start(bf16[1,4,6,1024]{3,2,1,0:T(8,128)(2,1)S(1)} %get-tuple-element.21), channel_id=1, source_target_pairs={{0,1},{2,3},{4,5},{6,7},{8,9},{10,11},{12,13},{14,15},{16,17},{18,... | collective-permute-start | bytes 147464 | tf_op jit(solution)/shard_map/ppermute | solution.py:17
  5.2 4.3 %fusion.83 = (f32[1024,1024]{1,0:T(8,128)}, f32[1024,1024]{1,0:T(8,128)}) fusion(), kind=kLoop, calls=%fused_computation.132 | loop fusion | flops 6291456 | bytes 8388608 | tf_op jit(solution)/shard_map/convert_element_type | solution.py:42
  9.5 4.3 %fusion.85 = (f32[1024,1024]{1,0:T(8,128)}, f32[1024,1024]{1,0:T(8,128)}) fusion(), kind=kLoop, calls=%fused_computation.134 | loop fusion | flops 6291456 | bytes 8388608 | tf_op jit(solution)/shard_map/convert_element_type | solution.py:42
  13.8 4.3 %fusion.87 = (f32[1024,1024]{1,0:T(8,128)}, f32[1024,1024]{1,0:T(8,128)}) fusion(), kind=kLoop, calls=%fused_computation.136 | loop fusion | flops 6291456 | bytes 8388608 | tf_op jit(solution)/shard_map/convert_element_type | solution.py:42
  18.2 2.5 %fusion.89 = f32[1024,1024]{1,0:T(8,128)} fusion(), kind=kLoop, calls=%fused_computation.138 | loop fusion | flops 4194304 | bytes 4194304 | tf_op jit(solution)/shard_map/convert_element_type | solution.py:42
  21.1 23.9 %fusion.96 = f32[1,4,268,1024]{3,2,1,0:T(8,128)S(1)} fusion(bf16[1,4,6,1024]{3,2,1,0:T(8,128)(2,1)S(1)} %collective-permute-done.1, bf16[1,4,256,1024]{3,2,1,0:T(8,128)(2,1)S(1)} %copy-done.1, bf16[1,4,6,1024]{3,2,1,0:T(8,128)(2,1)S(1)} %collective-permute-done, f32[1024,1024]{1,0:T(8,128)} %fusion.89, f32[4]{0:T(128)S(1)} %get-tuple-element.11, ...), kind=kOutput, calls=%fused_computation.152 | convolution fusion | flops 13549993984 | bytes 35946608 | tf_op jit(solution)/shard_map/tbrc,bcd->tbrd/dot_general | solution.py:43
  45.1 3.8 %fusion.29 = f32[1,4,262,1024]{3,2,1,0:T(8,128)S(1)} fusion(f32[1,4,268,1024]{3,2,1,0:T(8,128)S(1)} %fusion.96, f32[4]{0:T(128)S(1)} %get-tuple-element.42, f32[4]{0:T(128)S(1)} %get-tuple-element.41, f32[4]{0:T(128)S(1)} %get-tuple-element.40, f32[4]{0:T(128)S(1)} %get-tuple-element.39, f32[4]{0:T(128)S(1)} %get-tuple-element.38, ...), kind=kLoop, calls=%fused_computation.66 | loop fusion | flops 15024128 | bytes 34341240 | tf_op jit(solution)/shard_map/jit(_where)/select_n | solution.py:79
  48.9 2.8 %copy.24 = f32[1,4,262,1024]{3,1,2,0:T(4,128)S(1)} copy(f32[1,4,262,1024]{3,2,1,0:T(8,128)S(1)} %fusion.29) | data formatting | bytes 8585216 | tf_op jit(solution)/shard_map/jit(_where)/select_n | solution.py:79
  52.7 2.3 %fusion.100 = f32[4,130,1024]{2,0,1:T(4,128)S(1)} fusion(f32[1,4,131,1024]{3,1,2,0:T(4,128)S(1)} %get-tuple-element.18, f32[1,4,131,1024]{3,1,2,0:T(4,128)S(1)} %get-tuple-element.17), kind=kLoop, calls=%fused_computation.157 | loop fusion | flops 3727360 | bytes 10649600 | tf_op jit(solution)/shard_map/reshape.35
  55.0 5.7 %fusion.119 = f32[4,130,512]{2,1,0:T(8,128)S(1)} fusion(f32[4,130,1024]{2,0,1:T(4,128)S(1)} %fusion.100, s32[512]{0:T(512)S(1)} %iota_multiply_fusion, pred[130]{0:T(512)(128)(4,1)S(1)} %compare_and_fusion), kind=kOutput, calls=%fused_computation.182 | convolution fusion | flops 3278639104 | bytes 3197058 | tf_op jit(solution)/shard_map/dot_general | solution.py:56
  63.5 6.7 %all-to-all-start.2 = ((bf16[1,4,64,256]{3,1,0,2:T(4,128)(2,1)}), bf16[1,4,64,256]{3,1,0,2:T(4,128)(2,1)S(1)}, u32[]{:S(2)}, u32[]{:S(2)}) async-start(bf16[1,4,64,256]{3,1,0,2:T(4,128)(2,1)} %copy.32), calls=%async_computation.2 | async-start | bytes 262144 | tf_op jit(solution)/shard_map/all_to_all | solution.py:133
  71.6 6.8 %all-to-all-done.2 = bf16[1,4,64,256]{3,1,0,2:T(4,128)(2,1)S(1)} async-done(((bf16[1,4,64,256]{3,1,0,2:T(4,128)(2,1)}), bf16[1,4,64,256]{3,1,0,2:T(4,128)(2,1)S(1)}, u32[]{:S(2)}, u32[]{:S(2)}) %all-to-all-start.2) | async-done | bytes 131104 | tf_op jit(solution)/shard_map/all_to_all | solution.py:133
  78.4 3.5 %all-to-all-start.1 = ((bf16[1,4,128,512]{3,1,0,2:T(4,128)(2,1)}), bf16[1,4,128,512]{3,1,0,2:T(4,128)(2,1)S(1)}, u32[]{:S(2)}, u32[]{:S(2)}) async-start(bf16[1,4,128,512]{3,1,0,2:T(4,128)(2,1)} %copy.27), calls=%async_computation.1 | async-start | bytes 1048576 | tf_op jit(solution)/shard_map/all_to_all | solution.py:130
  82.2 2.8 %slice.1298 = bf16[1,4,256,1024]{3,2,1,0:T(8,128)(2,1)S(1)} slice(f32[1,4,262,1024]{3,2,1,0:T(8,128)} %copy-done), slice={[0:1], [0:4], [3:259], [0:1024]} | slice | bytes 4194304 | tf_op jit(solution)/shard_map/slice | solution.py:117
  85.0 2.9 %copy.22 = bf16[1,4,256,1024]{3,1,0,2:T(4,128)(2,1)} copy(bf16[1,4,256,1024]{3,2,1,0:T(8,128)(2,1)S(1)} %slice.1298) | data formatting | bytes 4194304 | tf_op jit(solution)/shard_map/slice | solution.py:117
  88.0 8.6 %all-to-all-done.1 = bf16[1,4,128,512]{3,1,0,2:T(4,128)(2,1)S(1)} async-done(((bf16[1,4,128,512]{3,1,0,2:T(4,128)(2,1)}), bf16[1,4,128,512]{3,1,0,2:T(4,128)(2,1)S(1)}, u32[]{:S(2)}, u32[]{:S(2)}) %all-to-all-start.1) | async-done | bytes 524320 | tf_op jit(solution)/shard_map/all_to_all | solution.py:130
  96.6 4.6 %all-to-all-start = ((bf16[1,4,256,1024]{3,1,0,2:T(4,128)(2,1)}), bf16[1,4,256,1024]{3,1,0,2:T(4,128)(2,1)}, u32[]{:S(2)}, u32[]{:S(2)}) async-start(bf16[1,4,256,1024]{3,1,0,2:T(4,128)(2,1)} %copy.22), calls=%async_computation | async-start | bytes 4194304 | tf_op jit(solution)/shard_map/all_to_all | solution.py:127
  104.2 1.4 add.471
  110.7 2.0 %fusion.129 = bf16[8,4,16,512]{3,2,1,0:T(8,128)(2,1)} fusion(f32[8,4,16,512]{3,2,1,0:T(8,128)S(1)} %fusion.182, f32[4,4,16,512]{3,2,1,0:T(8,128)S(1)} %reshape.284, f32[4,4,16,512]{3,2,1,0:T(8,128)S(1)} %reshape.283), kind=kLoop, calls=%fused_computation.205 | loop fusion | flops 6815744 | bytes 2621440 | tf_op jit(solution)/shard_map/convert_element_type | solution.py:99
  112.7 36.2 %all-to-all-done = bf16[1,4,256,1024]{3,1,0,2:T(4,128)(2,1)} async-done(((bf16[1,4,256,1024]{3,1,0,2:T(4,128)(2,1)}), bf16[1,4,256,1024]{3,1,0,2:T(4,128)(2,1)}, u32[]{:S(2)}, u32[]{:S(2)}) %all-to-all-start) | async-done | bytes 2097184 | tf_op jit(solution)/shard_map/all_to_all | solution.py:127
  149.0 2.8 %convert.18 = f32[1,4,8,32,1024]{4,1,3,2,0:T(4,128)S(1)} convert(bf16[1,4,8,32,1024]{4,1,3,2,0:T(4,128)(2,1)} %bitcast.43) | non-fusion elementwise | flops 1048576 | bytes 6291456 | tf_op jit(solution)/shard_map/convert_element_type | solution.py:83
  151.8 4.5 %bitcast_multiply_fusion = f32[8,4,32,1024]{3,2,1,0:T(8,128)} fusion(f32[1,4,8,32,1024]{4,1,3,2,0:T(4,128)S(1)} %convert.18, f32[8,32,1024]{2,1,0:T(8,128)S(1)} %get-tuple-element.28), kind=kLoop, calls=%fused_computation.121 | loop fusion | flops 1048576 | bytes 9437184 | tf_op jit(solution)/shard_map/mul | solution.py:87
  156.4 13.9 %fusion.75 = f32[8,4,32,1024]{3,2,1,0:T(8,128)S(1)} fusion(f32[8,4,32,1024]{3,2,1,0:T(8,128)} %bitcast_multiply_fusion, f32[1,4,8,32,1024]{4,1,3,2,0:T(4,128)S(1)} %convert.18, f32[8,32,1024]{2,1,0:T(8,128)} %fusion.155, f32[8,32,1024]{2,1,0:T(8,128)} %get-tuple-element.27, f32[8,32,1024]{2,1,0:T(8,128)S(1)} %convert_element_type.202), kind=kLoop, calls=%fused_computation.123 | loop fusion | flops 20971520 | bytes 15728640 | tf_op jit(solution)/shard_map/add | solution.py:94
  170.9 5.8 %fusion.39 = bf16[8,4,32,1024]{3,2,1,0:T(8,128)(2,1)} fusion(f32[8,4,32,1024]{3,2,1,0:T(8,128)S(1)} %fusion.75, f32[4,4,32,1024]{3,2,1,0:T(8,128)S(1)} %reshape.280, f32[4,4,32,1024]{3,2,1,0:T(8,128)S(1)} %reshape.279), kind=kLoop, calls=%fused_computation.82 | loop fusion | flops 27262976 | bytes 10485760 | tf_op jit(solution)/shard_map/convert_element_type | solution.py:99
  (70 shorter events, 16.6 us)
Async XLA Ops:
  1.5 19.6 %collective-permute-start = (bf16[1,4,6,1024]{3,2,1,0:T(8,128)(2,1)S(1)}, bf16[1,4,6,1024]{3,2,1,0:T(8,128)(2,1)S(1)}, u32[]{:S(2)}, u32[]{:S(2)}) collective-permute-start(bf16[1,4,6,1024]{3,2,1,0:T(8,128)(2,1)S(1)} %get-tuple-element.21), channel_id=1, source_target_pairs={{0,1},{2,3},{4,5},{6,7},{8,9},{10,11},{12,13},{14,15},{16,17},{18,... | collective-permute-start | bytes 147464 | tf_op jit(solution)/shard_map/ppermute | solution.py:17
  3.9 17.2 %collective-permute-start.1 = (bf16[1,4,6,1024]{3,2,1,0:T(8,128)(2,1)S(1)}, bf16[1,4,6,1024]{3,2,1,0:T(8,128)(2,1)S(1)}, u32[]{:S(2)}, u32[]{:S(2)}) collective-permute-start(bf16[1,4,6,1024]{3,2,1,0:T(8,128)(2,1)S(1)} %get-tuple-element.22), channel_id=1, source_target_pairs={{1,0},{3,2},{5,4},{7,6},{9,8},{11,10},{13,12},{15,14},{17,16},{19,... | collective-permute-start | bytes 147464 | tf_op jit(solution)/shard_map/ppermute | solution.py:20
  18.2 2.5 %copy-start.5 = (f32[2,4,7]{2,1,0:T(4,128)S(1)}, f32[2,4,7]{2,1,0:T(4,128)}, u32[]{:S(2)}) copy-start(f32[2,4,7]{2,1,0:T(4,128)} %param.4) | copy-start | bytes 676
  18.2 2.9 %copy-start.1 = (bf16[1,4,256,1024]{3,2,1,0:T(8,128)(2,1)S(1)}, bf16[1,4,256,1024]{3,2,1,0:T(8,128)(2,1)}, u32[]{:S(2)}) copy-start(bf16[1,4,256,1024]{3,2,1,0:T(8,128)(2,1)} %param.3) | copy-start | bytes 6291460
  48.9 2.8 %copy-start = (f32[1,4,262,1024]{3,2,1,0:T(8,128)}, f32[1,4,262,1024]{3,2,1,0:T(8,128)S(1)}, u32[]{:S(2)}) copy-start(f32[1,4,262,1024]{3,2,1,0:T(8,128)S(1)} %fusion.29) | copy-start | bytes 12877828
  61.9 20.0 %copy-start.4 = (s32[8,8,8]{2,1,0:T(8,128)S(1)}, s32[8,8,8]{2,1,0:T(8,128)}, u32[]{:S(2)}) copy-start(s32[8,8,8]{2,1,0:T(8,128)} %param.5) | copy-start | bytes 6148
  63.5 14.9 %all-to-all-start.2 = ((bf16[1,4,64,256]{3,1,0,2:T(4,128)(2,1)}), bf16[1,4,64,256]{3,1,0,2:T(4,128)(2,1)S(1)}, u32[]{:S(2)}, u32[]{:S(2)}) async-start(bf16[1,4,64,256]{3,1,0,2:T(4,128)(2,1)} %copy.32), calls=%async_computation.2 | async-start | bytes 262144 | tf_op jit(solution)/shard_map/all_to_all | solution.py:133
  78.4 9.6 %copy-start.2 = (bf16[1,4,64,256]{3,1,0,2:T(4,128)(2,1)}, bf16[1,4,64,256]{3,1,0,2:T(4,128)(2,1)S(1)}, u32[]{:S(2)}) copy-start(bf16[1,4,64,256]{3,1,0,2:T(4,128)(2,1)S(1)} %all-to-all-done.2) | copy-start | bytes 393220
  78.4 18.2 %all-to-all-start.1 = ((bf16[1,4,128,512]{3,1,0,2:T(4,128)(2,1)}), bf16[1,4,128,512]{3,1,0,2:T(4,128)(2,1)S(1)}, u32[]{:S(2)}, u32[]{:S(2)}) async-start(bf16[1,4,128,512]{3,1,0,2:T(4,128)(2,1)} %copy.27), calls=%async_computation.1 | async-start | bytes 1048576 | tf_op jit(solution)/shard_map/all_to_all | solution.py:130
  96.6 52.4 %all-to-all-start = ((bf16[1,4,256,1024]{3,1,0,2:T(4,128)(2,1)}), bf16[1,4,256,1024]{3,1,0,2:T(4,128)(2,1)}, u32[]{:S(2)}, u32[]{:S(2)}) async-start(bf16[1,4,256,1024]{3,1,0,2:T(4,128)(2,1)} %copy.22), calls=%async_computation | async-start | bytes 4194304 | tf_op jit(solution)/shard_map/all_to_all | solution.py:127
  104.2 4.2 %copy-start.3 = (bf16[1,4,64,256]{3,1,0,2:T(4,128)(2,1)S(1)}, bf16[1,4,64,256]{3,1,0,2:T(4,128)(2,1)}, u32[]{:S(2)}) copy-start(bf16[1,4,64,256]{3,1,0,2:T(4,128)(2,1)} %copy-done.2) | copy-start | bytes 393220
where the time goes:
time: 180 us; the launch traced here: 177 us
  other arithmetic  56 us (31%)
  waiting for transfers between devices  51.7 us (29%)
  matrix products  30.5 us (17%)
  local copies, waits for them, and re-layouts  19 us (11%)
  starting transfers between devices  18.4 us (10%)
    all_to_all x1, waiting for transfers between devices, local(): lax.all_to_all(level_zero, 'date', split_axis=2, concat_axis=0, tiled=True)  36.2 us
    dot_general x1, matrix products, column_resample(): jnp.einsum('tbrc,bcd->tbrd', values.astype(jnp.float32), table, precision...  23.9 us
    convert_element_type x4, other arithmetic, column_resample(): (offset == k).astype(jnp.float32)[None]  15.4 us
    add x3, other arithmetic, smooth(): filled = clear4 * values + (1.0 - clear4) * (numer / denom)  14.7 us
    convert_element_type x3, other arithmetic, smooth(): return result.astype(jnp.bfloat16)  8.65 us
    all_to_all x1, waiting for transfers between devices, local(): lax.all_to_all(level_one, 'date', split_axis=2, concat_axis=0, tiled=True)  8.64 us
    all_to_all x1, waiting for transfers between devices, local(): lax.all_to_all(level_two, 'date', split_axis=2, concat_axis=0, tiled=True)  6.81 us
    all_to_all x1, starting transfers between devices, local(): lax.all_to_all(level_two, 'date', split_axis=2, concat_axis=0, tiled=True)  6.67 us
  transfers between devices with their start and end apart: 5, of which 3 were waited for; matrix products, arithmetic and copies ran while one was open for 20% of the time, Pallas kernels for 0%

commit v1 on v0

--- a/solution.py
+++ b/solution.py
@@ -7,6 +7,13 @@
 gap_weights = [math.exp(-((k - 4) ** 2) / 8.0) for k in range(9)]
 savgol_coeffs = [c / 231.0 for c in [-21.0, 14.0, 39.0, 54.0, 59.0, 54.0, 39.0, 14.0, -21.0]]
 pyramid_filter = [0.125, 0.375, 0.375, 0.125]
+
+
+def trade_parts(block, axis, split, join):
+    size = lax.axis_size(axis)
+    blocks = jnp.stack(jnp.split(block, size, axis=split), axis=0)
+    blocks = lax.all_to_all(blocks, axis, split_axis=0, concat_axis=0)
+    return jnp.concatenate(blocks, axis=join)
 
 
 def padded(block, sides, width):
@@ -123,9 +130,7 @@
     clear_fine = expand_mask(clear_mask, 4, 128)
     clear_half = expand_mask(clear_mask, 2, 64)
     clear_quarter = expand_mask(clear_mask, 1, 32)
-    smooth_fine = smooth(
-        lax.all_to_all(level_zero, "date", split_axis=2, concat_axis=0, tiled=True), clear_fine
-    )
+    smooth_fine = smooth(trade_parts(level_zero, "date", 2, 0), clear_fine)
     smooth_half = smooth(
         lax.all_to_all(level_one, "date", split_axis=2, concat_axis=0, tiled=True), clear_half
     )

time: 180 us -> 163 us (0.906); the launches traced: 177 us -> 162 us
  waiting for transfers between devices: 51.7 us -> 37 us
  local copies, waits for them, and re-layouts: 19 us -> 27.2 us
  other arithmetic: 56 us -> 49.4 us
    all_to_all x1, waiting for transfers between devices: 36.2 us -> 21.6 us  [trade_parts(): blocks = lax.all_to_all(blocks, axis, split_axis=0, concat_axis=0)]
    add x3, other arithmetic: 14.7 us -> 6 us  [smooth(): filled = clear4 * values + (1.0 - clear4) * (numer / denom)]
    div x3, other arithmetic: 1.48 us -> 8.49 us  [smooth(): filled = clear4 * values + (1.0 - clear4) * (numer / denom)]
    slice x2 -> x0, local copies, waits for them, and re-layouts: 5.77 us -> none  [local(): resampled = resampled_wide[:, :, 3:3 + rows]]
    unnamed x12 -> x25, local copies, waits for them, and re-layouts: 0.03 us -> 5.45 us
    another operation x2 -> x3, other arithmetic: 2.58 us -> 6.55 us
    select_n x2 -> x1, other arithmetic: 3.91 us -> 0.07 us  [keep_rows(): return jnp.where(inside[None, None, :, None], values, 0.0)]
    all_to_all x1, waiting for transfers between devices: 6.81 us -> 3.79 us  [local(): lax.all_to_all(level_two, 'date', split_axis=2, concat_axis=0, tiled=True)]
  transfers between devices with their start and end apart: 5 -> 5, of which waited for: 3 -> 3; matrix products, arithmetic and copies ran while one was open for 20% -> 31% of each run, Pallas kernels for 0% -> 0%
where the time goes in v1:
time: 163 us; the launch traced here: 162 us
  other arithmetic  49.4 us (30%)
  waiting for transfers between devices  37 us (23%)
  matrix products  30.2 us (19%)
  local copies, waits for them, and re-layouts  27.2 us (17%)
  starting transfers between devices  17.7 us (11%)
    dot_general x1, matrix products, column_resample(): jnp.einsum('tbrc,bcd->tbrd', values.astype(jnp.float32), table, precision...  23.6 us
    all_to_all x1, waiting for transfers between devices, trade_parts(): blocks = lax.all_to_all(blocks, axis, split_axis=0, concat_axis=0)  21.6 us
    convert_element_type x4, other arithmetic, column_resample(): (offset == k).astype(jnp.float32)[None]  15.4 us
    all_to_all x1, waiting for transfers between devices, local(): lax.all_to_all(level_one, 'date', split_axis=2, concat_axis=0, tiled=True)  11.6 us
    convert_element_type x3, other arithmetic, smooth(): return result.astype(jnp.bfloat16)  8.5 us
    div x3, other arithmetic, smooth(): filled = clear4 * values + (1.0 - clear4) * (numer / denom)  8.49 us
    all_to_all x1, starting transfers between devices, local(): lax.all_to_all(level_two, 'date', split_axis=2, concat_axis=0, tiled=True)  6.66 us
    dot_general x2, matrix products, halve_columns(): return jnp.dot(values, table, precision=lax.Precision.HIGHEST)  6.56 us
  transfers between devices with their start and end apart: 5, of which 3 were waited for; matrix products, arithmetic and copies ran while one was open for 31% of the time, Pallas kernels for 0%

profile of v1, /device:TPU:0, one launch (start us, length us, event | category | flops | bytes accessed | tf_op | source)
XLA Modules:
  0.0 162.5 jit_solution(9615387475312363810)
XLA Ops:
  1.5 2.4 %collective-permute-start = (bf16[1,4,6,1024]{3,2,1,0:T(8,128)(2,1)S(1)}, bf16[1,4,6,1024]{3,2,1,0:T(8,128)(2,1)S(1)}, u32[]{:S(2)}, u32[]{:S(2)}) collective-permute-start(bf16[1,4,6,1024]{3,2,1,0:T(8,128)(2,1)S(1)} %get-tuple-element.23), channel_id=1, source_target_pairs={{0,1},{2,3},{4,5},{6,7},{8,9},{10,11},{12,13},{14,15},{16,17},{18,... | collective-permute-start | bytes 147464 | tf_op jit(solution)/shard_map/ppermute | solution.py:24
  5.2 4.3 %fusion.83 = (f32[1024,1024]{1,0:T(8,128)}, f32[1024,1024]{1,0:T(8,128)}) fusion(), kind=kLoop, calls=%fused_computation.131 | loop fusion | flops 6291456 | bytes 8388608 | tf_op jit(solution)/shard_map/convert_element_type | solution.py:49
  9.5 4.3 %fusion.85 = (f32[1024,1024]{1,0:T(8,128)}, f32[1024,1024]{1,0:T(8,128)}) fusion(), kind=kLoop, calls=%fused_computation.133 | loop fusion | flops 6291456 | bytes 8388608 | tf_op jit(solution)/shard_map/convert_element_type | solution.py:49
  13.8 4.3 %fusion.87 = (f32[1024,1024]{1,0:T(8,128)}, f32[1024,1024]{1,0:T(8,128)}) fusion(), kind=kLoop, calls=%fused_computation.135 | loop fusion | flops 6291456 | bytes 8388608 | tf_op jit(solution)/shard_map/convert_element_type | solution.py:49
  18.2 2.5 %fusion.89 = f32[1024,1024]{1,0:T(8,128)} fusion(), kind=kLoop, calls=%fused_computation.137 | loop fusion | flops 4194304 | bytes 4194304 | tf_op jit(solution)/shard_map/convert_element_type | solution.py:49
  21.4 23.6 %fusion.96 = f32[1,4,268,1024]{3,2,1,0:T(8,128)S(1)} fusion(bf16[1,4,6,1024]{3,2,1,0:T(8,128)(2,1)S(1)} %collective-permute-done.1, bf16[1,4,256,1024]{3,2,1,0:T(8,128)(2,1)S(1)} %copy-done.1, bf16[1,4,6,1024]{3,2,1,0:T(8,128)(2,1)S(1)} %collective-permute-done, f32[1024,1024]{1,0:T(8,128)} %fusion.89, f32[4]{0:T(128)S(1)} %get-tuple-element.11, ...), kind=kOutput, calls=%fused_computation.151 | convolution fusion | flops 13549993984 | bytes 35946608 | tf_op jit(solution)/shard_map/tbrc,bcd->tbrd/dot_general | solution.py:50
  45.1 3.9 %fusion.321 = (bf16[1,4,262,1024]{3,2,1,0:T(8,128)(2,1)S(1)}, f32[1,4,262,1024]{3,2,1,0:T(8,128)S(1)}) fusion(f32[1,4,268,1024]{3,2,1,0:T(8,128)S(1)} %fusion.96, f32[4]{0:T(128)S(1)} %get-tuple-element.44, f32[4]{0:T(128)S(1)} %get-tuple-element.43, f32[4]{0:T(128)S(1)} %get-tuple-element.42, f32[4]{0:T(128)S(1)} %get-tuple-element.41, ...), kind=kLoop, calls=%fused_computation.469 | loop fusion | flops 16097280 | bytes 36487544 | tf_op jit(solution)/shard_map/convert.9
  49.0 2.8 %copy.20 = f32[1,4,262,1024]{3,1,2,0:T(4,128)S(1)} copy(f32[1,4,262,1024]{3,2,1,0:T(8,128)S(1)} %get-tuple-element.18) | data formatting | bytes 8585216 | tf_op jit(solution)/shard_map/jit(_where)/select_n | solution.py:86
  52.7 2.3 %fusion.100 = f32[4,130,1024]{2,0,1:T(4,128)S(1)} fusion(f32[1,4,131,1024]{3,1,2,0:T(4,128)S(1)} %get-tuple-element.20, f32[1,4,131,1024]{3,1,2,0:T(4,128)S(1)} %get-tuple-element.19), kind=kLoop, calls=%fused_computation.156 | loop fusion | flops 3727360 | bytes 10649600 | tf_op jit(solution)/shard_map/reshape.36
  55.1 5.7 %fusion.119 = f32[4,130,512]{2,1,0:T(8,128)S(1)} fusion(f32[4,130,1024]{2,0,1:T(4,128)S(1)} %fusion.100, s32[512]{0:T(512)S(1)} %iota_multiply_fusion, pred[130]{0:T(512)(128)(4,1)S(1)} %compare_and_fusion), kind=kOutput, calls=%fused_computation.181 | convolution fusion | flops 3278639104 | bytes 3197058 | tf_op jit(solution)/shard_map/dot_general | solution.py:63
  63.7 6.7 %all-to-all-start.2 = ((bf16[1,4,64,256]{3,1,0,2:T(4,128)(2,1)}), bf16[1,4,64,256]{3,1,0,2:T(4,128)(2,1)S(1)}, u32[]{:S(2)}, u32[]{:S(2)}) async-start(bf16[1,4,64,256]{3,1,0,2:T(4,128)(2,1)} %copy.28), calls=%async_computation.2 | async-start | bytes 262144 | tf_op jit(solution)/shard_map/all_to_all | solution.py:138
  74.8 3.8 %all-to-all-done.2 = bf16[1,4,64,256]{3,1,0,2:T(4,128)(2,1)S(1)} async-done(((bf16[1,4,64,256]{3,1,0,2:T(4,128)(2,1)}), bf16[1,4,64,256]{3,1,0,2:T(4,128)(2,1)S(1)}, u32[]{:S(2)}, u32[]{:S(2)}) %all-to-all-start.2) | async-done | bytes 131104 | tf_op jit(solution)/shard_map/all_to_all | solution.py:138
  78.6 3.5 %all-to-all-start.1 = ((bf16[1,4,128,512]{3,1,0,2:T(4,128)(2,1)}), bf16[1,4,128,512]{3,1,0,2:T(4,128)(2,1)S(1)}, u32[]{:S(2)}, u32[]{:S(2)}) async-start(bf16[1,4,128,512]{3,1,0,2:T(4,128)(2,1)} %copy.23), calls=%async_computation.1 | async-start | bytes 1048576 | tf_op jit(solution)/shard_map/all_to_all | solution.py:135
  85.2 11.6 %all-to-all-done.1 = bf16[1,4,128,512]{3,1,0,2:T(4,128)(2,1)S(1)} async-done(((bf16[1,4,128,512]{3,1,0,2:T(4,128)(2,1)}), bf16[1,4,128,512]{3,1,0,2:T(4,128)(2,1)S(1)}, u32[]{:S(2)}, u32[]{:S(2)}) %all-to-all-start.1) | async-done | bytes 524320 | tf_op jit(solution)/shard_map/all_to_all | solution.py:135
  96.8 3.9 %all-to-all-start = ((bf16[8,1,4,32,1024]{4,3,2,1,0:T(8,128)(2,1)}), bf16[8,1,4,32,1024]{4,3,2,1,0:T(8,128)(2,1)S(1)}, u32[]{:S(2)}, u32[]{:S(2)}) async-start(bf16[8,1,4,32,1024]{4,3,2,1,0:T(8,128)(2,1)} %fusion.269), calls=%async_computation | async-start | bytes 4194304 | tf_op jit(solution)/shard_map/all_to_all | solution.py:15
  104.8 1.9 %add.509 = f32[8,1,16,512]{3,2,0,1:T(8,128)} reshape(f32[8,16,8,64]{3,2,1,0:T(8,128)} %broadcast_in_dim.84) | data formatting | bytes 524288 | tf_op jit(solution)/shard_map/add | solution.py:93
  110.9 2.4 %add.471 = f32[8,1,32,1024]{3,2,0,1:T(8,128)} reshape(f32[8,32,8,128]{3,2,1,0:T(8,128)} %broadcast_in_dim.78) | data formatting | bytes 2097152 | tf_op jit(solution)/shard_map/add | solution.py:93
  113.3 1.9 %fusion.242 = f32[8,16,512]{2,1,0:T(8,128)S(1)} fusion(f32[8,1,16,512]{3,2,0,1:T(8,128)} %add.509), kind=kLoop, calls=%fused_computation.349 | loop fusion | flops 1048576 | bytes 524288 | tf_op jit(solution)/shard_map/div | solution.py:101
  115.3 5.9 %fusion.155 = f32[8,32,1024]{2,1,0:T(8,128)} fusion(f32[8,1,32,1024]{3,2,0,1:T(8,128)} %add.471), kind=kLoop, calls=%fused_computation.230 | loop fusion | flops 4194304 | bytes 2097152 | tf_op jit(solution)/shard_map/div | solution.py:101
  125.3 2.0 %fusion.129 = bf16[8,4,16,512]{3,2,1,0:T(8,128)(2,1)} fusion(f32[8,4,16,512]{3,2,1,0:T(8,128)S(1)} %fusion.182, f32[4,4,16,512]{3,2,1,0:T(8,128)S(1)} %reshape.283, f32[4,4,16,512]{3,2,1,0:T(8,128)S(1)} %reshape.282), kind=kLoop, calls=%fused_computation.204 | loop fusion | flops 6815744 | bytes 2621440 | tf_op jit(solution)/shard_map/convert_element_type | solution.py:106
  127.3 21.6 %all-to-all-done = bf16[8,1,4,32,1024]{4,3,2,1,0:T(8,128)(2,1)S(1)} async-done(((bf16[8,1,4,32,1024]{4,3,2,1,0:T(8,128)(2,1)}), bf16[8,1,4,32,1024]{4,3,2,1,0:T(8,128)(2,1)S(1)}, u32[]{:S(2)}, u32[]{:S(2)}) %all-to-all-start) | async-done | bytes 2097184 | tf_op jit(solution)/shard_map/all_to_all | solution.py:15
  148.9 2.0 %convert_multiply_fusion = f32[8,4,32,1024]{3,2,1,0:T(8,128)S(1)} fusion(bf16[8,1,4,32,1024]{4,3,2,1,0:T(8,128)(2,1)S(1)} %all-to-all-done, f32[8,32,1024]{2,1,0:T(8,128)} %get-tuple-element.30), kind=kLoop, calls=%fused_computation.48 | loop fusion | flops 2097152 | bytes 7340032 | tf_op jit(solution)/shard_map/mul | solution.py:94
  150.9 5.2 %fusion.35 = f32[8,4,32,1024]{3,2,1,0:T(8,128)S(1)} fusion(f32[8,4,32,1024]{3,2,1,0:T(8,128)S(1)} %convert_multiply_fusion, bf16[8,1,4,32,1024]{4,3,2,1,0:T(8,128)(2,1)S(1)} %all-to-all-done, f32[8,32,1024]{2,1,0:T(8,128)} %fusion.155, f32[8,32,1024]{2,1,0:T(8,128)S(1)} %copy-done, f32[8,32,1024]{2,1,0:T(8,128)S(1)} %convert_element_type.196), kind=kLoop, calls=%fused_computation.80 | loop fusion | flops 22020096 | bytes 13631488 | tf_op jit(solution)/shard_map/add | solution.py:101
  156.8 5.7 %fusion.40 = bf16[8,4,32,1024]{3,2,1,0:T(8,128)(2,1)} fusion(f32[8,4,32,1024]{3,2,1,0:T(8,128)S(1)} %fusion.35, f32[4,4,32,1024]{3,2,1,0:T(8,128)S(1)} %reshape.279, f32[4,4,32,1024]{3,2,1,0:T(8,128)S(1)} %reshape.278), kind=kLoop, calls=%fused_computation.85 | loop fusion | flops 27262976 | bytes 10485760 | tf_op jit(solution)/shard_map/convert_element_type | solution.py:106
  (81 shorter events, 27.2 us)
Async XLA Ops:
  1.5 19.8 %collective-permute-start = (bf16[1,4,6,1024]{3,2,1,0:T(8,128)(2,1)S(1)}, bf16[1,4,6,1024]{3,2,1,0:T(8,128)(2,1)S(1)}, u32[]{:S(2)}, u32[]{:S(2)}) collective-permute-start(bf16[1,4,6,1024]{3,2,1,0:T(8,128)(2,1)S(1)} %get-tuple-element.23), channel_id=1, source_target_pairs={{0,1},{2,3},{4,5},{6,7},{8,9},{10,11},{12,13},{14,15},{16,17},{18,... | collective-permute-start | bytes 147464 | tf_op jit(solution)/shard_map/ppermute | solution.py:24
  3.9 17.5 %collective-permute-start.1 = (bf16[1,4,6,1024]{3,2,1,0:T(8,128)(2,1)S(1)}, bf16[1,4,6,1024]{3,2,1,0:T(8,128)(2,1)S(1)}, u32[]{:S(2)}, u32[]{:S(2)}) collective-permute-start(bf16[1,4,6,1024]{3,2,1,0:T(8,128)(2,1)S(1)} %get-tuple-element.24), channel_id=1, source_target_pairs={{1,0},{3,2},{5,4},{7,6},{9,8},{11,10},{13,12},{15,14},{17,16},{19,... | collective-permute-start | bytes 147464 | tf_op jit(solution)/shard_map/ppermute | solution.py:27
  18.2 2.5 %copy-start.8 = (f32[2,4,7]{2,1,0:T(4,128)S(1)}, f32[2,4,7]{2,1,0:T(4,128)}, u32[]{:S(2)}) copy-start(f32[2,4,7]{2,1,0:T(4,128)} %param.4) | copy-start | bytes 676
  18.2 2.5 %copy-start.7 = (s32[8,8,8]{2,1,0:T(8,128)S(1)}, s32[8,8,8]{2,1,0:T(8,128)}, u32[]{:S(2)}) copy-start(s32[8,8,8]{2,1,0:T(8,128)} %param.5) | copy-start | bytes 6148
  18.2 3.2 %copy-start.1 = (bf16[1,4,256,1024]{3,2,1,0:T(8,128)(2,1)S(1)}, bf16[1,4,256,1024]{3,2,1,0:T(8,128)(2,1)}, u32[]{:S(2)}) copy-start(bf16[1,4,256,1024]{3,2,1,0:T(8,128)(2,1)} %param.3) | copy-start | bytes 6291460
  63.7 14.9 %all-to-all-start.2 = ((bf16[1,4,64,256]{3,1,0,2:T(4,128)(2,1)}), bf16[1,4,64,256]{3,1,0,2:T(4,128)(2,1)S(1)}, u32[]{:S(2)}, u32[]{:S(2)}) async-start(bf16[1,4,64,256]{3,1,0,2:T(4,128)(2,1)} %copy.28), calls=%async_computation.2 | async-start | bytes 262144 | tf_op jit(solution)/shard_map/all_to_all | solution.py:138
  78.6 22.7 %copy-start.4 = (bf16[1,4,64,256]{3,1,0,2:T(4,128)(2,1)}, bf16[1,4,64,256]{3,1,0,2:T(4,128)(2,1)S(1)}, u32[]{:S(2)}) copy-start(bf16[1,4,64,256]{3,1,0,2:T(4,128)(2,1)S(1)} %all-to-all-done.2) | copy-start | bytes 393220
  78.6 18.2 %all-to-all-start.1 = ((bf16[1,4,128,512]{3,1,0,2:T(4,128)(2,1)}), bf16[1,4,128,512]{3,1,0,2:T(4,128)(2,1)S(1)}, u32[]{:S(2)}, u32[]{:S(2)}) async-start(bf16[1,4,128,512]{3,1,0,2:T(4,128)(2,1)} %copy.23), calls=%async_computation.1 | async-start | bytes 1048576 | tf_op jit(solution)/shard_map/all_to_all | solution.py:135
  96.8 10.0 %copy-start.2 = (bf16[1,4,128,512]{3,1,0,2:T(4,128)(2,1)}, bf16[1,4,128,512]{3,1,0,2:T(4,128)(2,1)S(1)}, u32[]{:S(2)}) copy-start(bf16[1,4,128,512]{3,1,0,2:T(4,128)(2,1)S(1)} %all-to-all-done.1) | copy-start | bytes 1572868
  96.8 52.1 %all-to-all-start = ((bf16[8,1,4,32,1024]{4,3,2,1,0:T(8,128)(2,1)}), bf16[8,1,4,32,1024]{4,3,2,1,0:T(8,128)(2,1)S(1)}, u32[]{:S(2)}, u32[]{:S(2)}) async-start(bf16[8,1,4,32,1024]{4,3,2,1,0:T(8,128)(2,1)} %fusion.269), calls=%async_computation | async-start | bytes 4194304 | tf_op jit(solution)/shard_map/all_to_all | solution.py:15
  113.3 9.6 %copy-start.5 = (bf16[1,4,64,256]{3,1,0,2:T(4,128)(2,1)S(1)}, bf16[1,4,64,256]{3,1,0,2:T(4,128)(2,1)}, u32[]{:S(2)}) copy-start(bf16[1,4,64,256]{3,1,0,2:T(4,128)(2,1)} %copy-done.4) | copy-start | bytes 393220
  113.3 9.7 %copy-start.6 = (f32[8,8,256]{2,1,0:T(8,128)S(1)}, f32[8,8,256]{2,1,0:T(8,128)}, u32[]{:S(2)}) copy-start(f32[8,8,256]{2,1,0:T(8,128)} %fusion.295) | copy-start | bytes 196612
  115.3 8.7 %copy-start.3 = (bf16[1,4,128,512]{3,1,0,2:T(4,128)(2,1)S(1)}, bf16[1,4,128,512]{3,1,0,2:T(4,128)(2,1)}, u32[]{:S(2)}) copy-start(bf16[1,4,128,512]{3,1,0,2:T(4,128)(2,1)} %copy-done.2) | copy-start | bytes 1572868
  148.9 2.0 %copy-start = (f32[8,32,1024]{2,1,0:T(8,128)S(1)}, f32[8,32,1024]{2,1,0:T(8,128)}, u32[]{:S(2)}) copy-start(f32[8,32,1024]{2,1,0:T(8,128)} %get-tuple-element.29) | copy-start | bytes 3145732
